TPU v7x, 256 devices: a whole 4x4x8 slice. The times are simulated.
256 devices in a mesh: row: 8 (over z), col: 32 (over y, x, core).
Axes of the slice: x: 4, y: 4, z: 8, core: 2. Of those that a mesh axis runs over, the one named last changes fastest.
Arguments:
- features: bfloat16 [32768, 128], P(('row', 'col')), may hold values from -6 to 6
- first_weight: bfloat16 [128, 512], replicated, may hold values from -0.5 to 0.5
- second_weight: bfloat16 [512, 128], replicated, may hold values from -0.25 to 0.25
- tile_rows: int32 [8, 32, 80], P('row', 'col'), may hold values from 0 to 31
- tile_cols: int32 [8, 32, 80], P('row', 'col'), may hold values from 0 to 7
- tile_live: int32 [8, 32], P('row', 'col'), may hold values from 1 to 80, as said below
- column_mask: int32 [8, 32, 80, 128], P('row', 'col'), may hold values 0 or 1
- edge_weight: bfloat16 [8, 32, 80, 128, 128], P('row', 'col'), may hold values from 0.049804688 to 1
- cotangent: bfloat16 [32768, 128], P(('row', 'col')), may hold values from -6 to 6
Outputs:
- output: bfloat16 [32768, 128], P(('row', 'col'))
- first_grad: float32 [128, 512], replicated
- second_grad: float32 [512, 128], replicated
Inputs may be any that keep to these rules, and one draw needn't show every extreme that they name: `tile_live`: slots at or past a device's count are unused; every device of the last column group of the grid uses all 80.
All inputs are finite; a program needn't handle non-finite values. No bound on the sum of `column_mask` on one device may be relied on, other than what follows from the above.
Results may differ from a plain program's by a relative error of at most 0.014.
Values may be sent and summed in bfloat16 or wider, within the bound.
No kernel may reach another device: no remote copies, remote signals or barrier semaphores. Data moves between devices by JAX's collectives and lax.ppermute only.
A program may use at most 128 MiB of HBM per device.

v0:
```python
import math
import jax
import jax.numpy as jnp
from jax import lax
from jax.sharding import PartitionSpec as P

BLOCK = 128
gelu_coef = math.sqrt(2.0 / math.pi)


def gelu_tanh(value):
    return 0.5 * value * (1.0 + jnp.tanh(gelu_coef * (value + 0.044715 * value * value * value)))


def gelu_slope(value):
    tanh_value = jnp.tanh(gelu_coef * (value + 0.044715 * value * value * value))
    return 0.5 * (1.0 + tanh_value) + 0.5 * value * (1.0 - tanh_value * tanh_value) * gelu_coef * (
        1.0 + 3.0 * 0.044715 * value * value
    )


def slot_batches(tile_values, target_index, source_index):
    slot_count = tile_values.shape[0]
    group_size = 16
    batches = slot_count // group_size
    return (
        tile_values.reshape(batches, group_size, BLOCK, BLOCK),
        target_index.reshape(batches, group_size),
        source_index.reshape(batches, group_size),
    )


def forward_part(tile_values, row_index, col_index, panel, target_blocks):
    feature_width = panel.shape[1]
    source_blocks = panel.reshape(-1, BLOCK, feature_width)

    def forward_accumulate(running, slot_piece):
        values_here, rows_here, cols_here = slot_piece
        contrib = jnp.einsum(
            "sij,sjf->sif",
            values_here,
            source_blocks[cols_here],
            preferred_element_type=jnp.float32,
        )
        return (running.at[rows_here].add(contrib), None)

    start = jnp.zeros((target_blocks, BLOCK, feature_width), jnp.float32)
    running, _ = lax.scan(
        forward_accumulate, start, slot_batches(tile_values, row_index, col_index)
    )
    return running.reshape(-1, feature_width)


def backward_part(tile_values, col_index, row_index, panel, target_blocks):
    feature_width = panel.shape[1]
    source_blocks = panel.reshape(-1, BLOCK, feature_width)

    def backward_accumulate(running, slot_piece):
        values_here, cols_here, rows_here = slot_piece
        contrib = jnp.einsum(
            "sij,sif->sjf",
            values_here,
            source_blocks[rows_here],
            preferred_element_type=jnp.float32,
        )
        return (running.at[cols_here].add(contrib), None)

    start = jnp.zeros((target_blocks, BLOCK, feature_width), jnp.float32)
    running, _ = lax.scan(
        backward_accumulate, start, slot_batches(tile_values, col_index, row_index)
    )
    return running.reshape(-1, feature_width)


def local(
    features,
    first_weight,
    second_weight,
    tile_rows,
    tile_cols,
    tile_live,
    column_mask,
    edge_weight,
    cotangent,
):
    slot_count = edge_weight.shape[2]
    node_count = features.shape[0]
    live_slots = (jnp.arange(slot_count, dtype=jnp.int32) < tile_live[0, 0]).astype(jnp.bfloat16)
    tile_values = (
        edge_weight[0, 0]
        * column_mask[0, 0].astype(jnp.bfloat16)[:, None, :]
        * live_slots[:, None, None]
    )
    row_index = tile_rows[0, 0]
    col_index = tile_cols[0, 0]
    row_groups = lax.axis_size("col") * node_count // BLOCK
    col_groups = lax.axis_size("row") * node_count // BLOCK
    row_sums = jnp.sum(tile_values.astype(jnp.float32), axis=2)
    degree_part = (
        jnp.zeros((row_groups, BLOCK), jnp.float32).at[row_index].add(row_sums).reshape(-1)
    )
    panel_in = lax.all_gather(features, "row", axis=0, tiled=True)
    partial_in = forward_part(tile_values, row_index, col_index, panel_in, row_groups)
    degree = lax.psum_scatter(degree_part, "col", scatter_dimension=0, tiled=True)
    summed_in = lax.psum_scatter(
        partial_in.astype(jnp.bfloat16), "col", scatter_dimension=0, tiled=True
    ).astype(jnp.float32)
    row_scale = (1.0 / jnp.sqrt(1.0 + degree))[:, None]
    first_mix = (features.astype(jnp.float32) + row_scale * summed_in).astype(jnp.bfloat16)
    first_pre = jnp.dot(first_mix, first_weight, preferred_element_type=jnp.float32)
    hidden = gelu_tanh(first_pre).astype(jnp.bfloat16)
    panel_hidden = lax.all_gather(hidden, "row", axis=0, tiled=True)
    partial_hidden = forward_part(tile_values, row_index, col_index, panel_hidden, row_groups)
    summed_hidden = lax.psum_scatter(
        partial_hidden.astype(jnp.bfloat16), "col", scatter_dimension=0, tiled=True
    ).astype(jnp.float32)
    second_mix = (hidden.astype(jnp.float32) + row_scale * summed_hidden).astype(jnp.bfloat16)
    output = jnp.dot(second_mix, second_weight, preferred_element_type=jnp.float32).astype(
        jnp.bfloat16
    )
    mix_grad = jnp.einsum("no,ho->nh", cotangent, second_weight, preferred_element_type=jnp.float32)
    scaled_grad = (row_scale * mix_grad).astype(jnp.bfloat16)
    grad_rows = lax.all_gather(scaled_grad, "col", axis=0, tiled=True)
    returned = lax.psum_scatter(
        backward_part(tile_values, col_index, row_index, grad_rows, col_groups).astype(
            jnp.bfloat16
        ),
        "row",
        scatter_dimension=0,
        tiled=True,
    ).astype(jnp.float32)
    hidden_grad = mix_grad + returned
    second_term = jnp.einsum("nh,no->ho", second_mix, cotangent, preferred_element_type=jnp.float32)
    pre_grad = (hidden_grad * gelu_slope(first_pre)).astype(jnp.bfloat16)
    first_term = jnp.einsum("ni,nh->ih", first_mix, pre_grad, preferred_element_type=jnp.float32)
    node_scale = 1.0 / math.sqrt(node_count * lax.axis_size("row") * lax.axis_size("col"))
    first_grad, second_grad = lax.psum(
        (first_term * node_scale, second_term * node_scale), ("row", "col")
    )
    return (output, first_grad, second_grad)


def solution(mesh):
    return jax.shard_map(
        local,
        mesh=mesh,
        in_specs=(
            P(("row", "col"), None),
            P(),
            P(),
            P("row", "col", None),
            P("row", "col", None),
            P("row", "col"),
            P("row", "col", None, None),
            P("row", "col", None, None, None),
            P(("row", "col"), None),
        ),
        out_specs=(P(("row", "col"), None), P(), P()),
        check_vma=False,
    )
```

profile of v0, /device:TPU:2, one launch (start us, length us, event | category | flops | bytes accessed | tf_op | source)
XLA Modules:
  0.0 728.3 jit_solution(3400894786560194901)
XLA Ops:
  12.0 28.8 %all_gather.9 = bf16[1024,128]{1,0:T(8,128)(2,1)S(1)} all-gather(bf16[128,128]{1,0:T(8,128)(2,1)} %param.15), channel_id=1, replica_groups=mesh['row'=8,'col'=32] {'row'}, dimensions={0}, use_global_device_ids=true | all-gather | bytes 294912 | tf_op jit(solution)/shard_map/all_gather | solution.py:102
  55.1 26.7 %while.30 = (s32[]{:T(128)}, f32[32,128,128]{2,1,0:T(8,128)}, s32[5,16]{1,0:T(8,128)S(1)}, bf16[5,16,128,128]{3,2,1,0:T(8,128)(2,1)}, s32[5,16]{1,0:T(8,128)S(1)}, /*index=5*/bf16[8,128,128]{2,1,0:T(8,128)(2,1)S(1)}, s32[]{:T(128)}) while((s32[]{:T(128)}, f32[32,128,128]{2,1,0:T(8,128)}, s32[5,16]{1,0:T(8,128)S(1)}, ...), condition=%wide.region_5.6_spmd, body=%wide.region_3.0_spmd.sunk | while | flops 67372128 | bytes 6296093 | solution.py:48
  88.8 119.0 %all-reduce = f32[4096]{0:T(1024)S(1)} all-reduce(f32[4096]{0:T(1024)S(1)} %bitcast.122), channel_id=2, replica_groups=mesh['row'=8,'col'=32] {'col'}, use_global_device_ids=true, to_apply=%region_2.3.clone | all-reduce | flops 4096 | bytes 32768
  210.6 36.8 %all-gather.3.cloned.1.call-done = bf16[1024,512]{1,0:T(8,128)(2,1)} async-done(((bf16[128,512]{1,0:T(8,128)(2,1)}), bf16[1024,512]{1,0:T(8,128)(2,1)}) %all-gather.3.cloned.1.call-update) | async-done | bytes 1048592 | tf_op jit(solution)/shard_map/all_gather | solution.py:112
  251.7 69.8 %while.31 = (s32[]{:T(128)}, f32[32,128,512]{2,1,0:T(8,128)}, s32[5,16]{1,0:T(8,128)S(1)}, bf16[5,16,128,128]{3,2,1,0:T(8,128)(2,1)}, s32[5,16]{1,0:T(8,128)S(1)}, /*index=5*/bf16[8,128,512]{2,1,0:T(8,128)(2,1)S(1)}, s32[]{:T(128)}) while((s32[]{:T(128)}, f32[32,128,512]{2,1,0:T(8,128)}, s32[5,16]{1,0:T(8,128)S(1)}, ...), condition=%wide.region_9.10_spmd, body=%wide.region_7.9_spmd.sunk | while | flops 269485152 | bytes 23597596 | solution.py:48
  256.1 9.5 %scatter_fusion.1 = f32[32,128,512]{2,1,0:T(8,128)} fusion(f32[32,128,512]{2,1,0:T(8,128)} %get-tuple-element.326, s32[16]{0:T(128)S(1)} %get-tuple-element.287, f32[16,128,512]{2,1,0:T(8,128)} %fusion.71), kind=kCustom, calls=%fused_computation.4.clone.1 | custom fusion | flops 1048576 | bytes 12582976 | tf_op jit(solution)/shard_map/while/body/eval_jaxpr/scatter-add | solution.py:45
  270.0 9.6 %scatter_fusion.1 = f32[32,128,512]{2,1,0:T(8,128)} fusion(f32[32,128,512]{2,1,0:T(8,128)} %get-tuple-element.326, s32[16]{0:T(128)S(1)} %get-tuple-element.287, f32[16,128,512]{2,1,0:T(8,128)} %fusion.71), kind=kCustom, calls=%fused_computation.4.clone.1 | custom fusion | flops 1048576 | bytes 12582976 | tf_op jit(solution)/shard_map/while/body/eval_jaxpr/scatter-add | solution.py:45
  284.0 9.6 %scatter_fusion.1 = f32[32,128,512]{2,1,0:T(8,128)} fusion(f32[32,128,512]{2,1,0:T(8,128)} %get-tuple-element.326, s32[16]{0:T(128)S(1)} %get-tuple-element.287, f32[16,128,512]{2,1,0:T(8,128)} %fusion.71), kind=kCustom, calls=%fused_computation.4.clone.1 | custom fusion | flops 1048576 | bytes 12582976 | tf_op jit(solution)/shard_map/while/body/eval_jaxpr/scatter-add | solution.py:45
  298.0 9.7 %scatter_fusion.1 = f32[32,128,512]{2,1,0:T(8,128)} fusion(f32[32,128,512]{2,1,0:T(8,128)} %get-tuple-element.326, s32[16]{0:T(128)S(1)} %get-tuple-element.287, f32[16,128,512]{2,1,0:T(8,128)} %fusion.71), kind=kCustom, calls=%fused_computation.4.clone.1 | custom fusion | flops 1048576 | bytes 12582976 | tf_op jit(solution)/shard_map/while/body/eval_jaxpr/scatter-add | solution.py:45
  312.1 9.5 %scatter_fusion.1 = f32[32,128,512]{2,1,0:T(8,128)} fusion(f32[32,128,512]{2,1,0:T(8,128)} %get-tuple-element.326, s32[16]{0:T(128)S(1)} %get-tuple-element.287, f32[16,128,512]{2,1,0:T(8,128)} %fusion.71), kind=kCustom, calls=%fused_computation.4.clone.1 | custom fusion | flops 1048576 | bytes 12582976 | tf_op jit(solution)/shard_map/while/body/eval_jaxpr/scatter-add | solution.py:45
  321.6 5.9 convert_element_type.91
  327.9 74.9 %while.32 = (s32[]{:T(128)}, f32[8,128,512]{2,1,0:T(8,128)S(1)}, s32[5,16]{1,0:T(8,128)S(1)}, bf16[5,16,128,128]{2,3,1,0:T(8,128)(2,1)}, s32[5,16]{1,0:T(8,128)S(1)}, /*index=5*/bf16[32,128,512]{2,1,0:T(8,128)(2,1)}, s32[]{:T(128)}) while((s32[]{:T(128)}, f32[8,128,512]{2,1,0:T(8,128)S(1)}, s32[5,16]{1,0:T(8,128)S(1)}, ...), condition=%wide.region_13.14_spmd, body=%wide.region_11.13_spmd.sunk | while | flops 269485152 | bytes 23597596 | solution.py:69
  336.5 6.2 scatter_fusion.2
  347.1 4.5 fusion.75
  351.6 6.3 scatter_fusion.2
  362.2 4.5 fusion.75
  366.6 6.1 scatter_fusion.2
  377.0 4.8 fusion.75
  381.8 6.2 scatter_fusion.2
  392.2 4.5 fusion.75
  396.7 6.1 scatter_fusion.2
  404.0 12.2 %reduce-scatter.6.cloned.1.call-done = bf16[128,512]{1,0:T(8,128)(2,1)} async-done(((bf16[4096,512]{1,0:T(8,128)(2,1)}), bf16[128,512]{1,0:T(8,128)(2,1)}) %reduce-scatter.6.cloned.1.call-update) | async-done | bytes 131088 | tf_op jit(solution)/shard_map/reduce_scatter | solution.py:114
  418.2 39.2 %reduce-scatter.8.cloned.1.call-done = bf16[128,512]{1,0:T(8,128)(2,1)} async-done(((bf16[1024,512]{1,0:T(8,128)(2,1)}), bf16[128,512]{1,0:T(8,128)(2,1)}) %reduce-scatter.8.cloned.1.call-update) | async-done | bytes 131088 | tf_op jit(solution)/shard_map/reduce_scatter | solution.py:124
  460.3 257.8 %all-reduce.4.cloned.1.call-done = (f32[128,512]{1,0:T(8,128)}, f32[512,128]{1,0:T(8,128)}) async-done(((f32[128,512]{1,0:T(8,128)}, f32[512,128]{1,0:T(8,128)}), (f32[128,512]{1,0:T(8,128)}, f32[512,128]{1,0:T(8,128)})) %all-reduce.4.cloned.1.call-update) | async-done | bytes 524304 | tf_op jit(solution)/shard_map/psum | solution.py:137
  (138 shorter events, 115.6 us)
Async XLA Ops:
  7.2 202.5 %copy-start = (bf16[512,128]{1,0:T(8,128)(2,1)S(1)}, bf16[512,128]{1,0:T(8,128)(2,1)}, u32[]{:S(2)}) copy-start(bf16[512,128]{1,0:T(8,128)(2,1)} %param.17) | copy-start | bytes 393220
  7.2 200.7 %reduce-scatter.4.cloned.1.call-start = ((), (), s32[]{:S(2)}) async-start(), calls=%async_computation.3 | async-start | bytes 1081344 | tf_op jit(solution)/shard_map/reduce_scatter | solution.py:105
  81.8 3.0 copy-start.15
  81.8 4.2 copy-start.14
  81.8 4.3 copy-start.5
  81.8 4.3 copy-start.2
  84.7 123.2 %copy-start.8 = (bf16[128,128]{1,0:T(8,128)(2,1)S(1)}, bf16[128,128]{1,0:T(8,128)(2,1)}, u32[]{:S(2)}) copy-start(bf16[128,128]{1,0:T(8,128)(2,1)} %param.15) | copy-start | bytes 98308
  84.7 123.2 %copy-start.12 = (bf16[128,512]{1,0:T(8,128)(2,1)S(1)}, bf16[128,512]{1,0:T(8,128)(2,1)}, u32[]{:S(2)}) copy-start(bf16[128,512]{1,0:T(8,128)(2,1)} %param.16) | copy-start | bytes 393220
  84.7 125.0 %copy-start.6 = (bf16[128,128]{1,0:T(8,128)(2,1)S(1)}, bf16[128,128]{1,0:T(8,128)(2,1)}, u32[]{:S(2)}) copy-start(bf16[128,128]{1,0:T(8,128)(2,1)} %param.23) | copy-start | bytes 98308
  84.7 162.7 %all-gather.3.cloned.1.call-start = ((), (), s32[]{:S(2)}) async-start(), calls=%async_computation.4 | async-start | bytes 1179648 | tf_op jit(solution)/shard_map/all_gather | solution.py:112
  207.9 43.9 %copy-start.10 = (f32[128]{0:T(128)}, f32[128]{0:T(128)S(1)}, u32[]{:S(2)}) copy-start(f32[128]{0:T(128)S(1)} %fusion.37) | copy-start | bytes 1540
  209.6 118.0 %all-gather.5.cloned.1.call-start = ((), (), s32[]{:S(2)}) async-start(), calls=%async_computation.6 | async-start | bytes 4325376 | tf_op jit(solution)/shard_map/all_gather | solution.py:123
  210.6 205.7 %reduce-scatter.6.cloned.1.call-start = ((), (), s32[]{:S(2)}) async-start(), calls=%async_computation.5 | async-start | bytes 4325376 | tf_op jit(solution)/shard_map/reduce_scatter | solution.py:114
  247.4 4.3 copy-start.1
  327.6 129.8 %reduce-scatter.8.cloned.1.call-start = ((), (), s32[]{:S(2)}) async-start(), calls=%async_computation.7 | async-start | bytes 1179648 | tf_op jit(solution)/shard_map/reduce_scatter | solution.py:124
  402.8 13.5 %copy-start.3 = (bf16[128,512]{1,0:T(8,128)(2,1)S(1)}, bf16[128,512]{1,0:T(8,128)(2,1)}, u32[]{:S(2)}) copy-start(bf16[128,512]{1,0:T(8,128)(2,1)} %get-tuple-element.170) | copy-start | bytes 393220
  402.8 13.4 %copy-start.7 = (bf16[128,128]{1,0:T(8,128)(2,1)S(1)}, bf16[128,128]{1,0:T(8,128)(2,1)}, u32[]{:S(2)}) copy-start(bf16[128,128]{1,0:T(8,128)(2,1)} %param.23) | copy-start | bytes 98308
  402.8 13.4 %copy-start.11 = (f32[128]{0:T(128)S(1)}, f32[128]{0:T(128)}, u32[]{:S(2)}) copy-start(f32[128]{0:T(128)} %copy-done.10) | copy-start | bytes 1540
  402.8 54.6 %copy-start.9 = (bf16[128,128]{1,0:T(8,128)(2,1)S(1)}, bf16[128,128]{1,0:T(8,128)(2,1)}, u32[]{:S(2)}) copy-start(bf16[128,128]{1,0:T(8,128)(2,1)} %param.15) | copy-start | bytes 98308
  402.8 54.5 %copy-start.13 = (bf16[128,128]{1,0:T(8,128)(2,1)S(1)}, bf16[128,128]{1,0:T(8,128)(2,1)}, u32[]{:S(2)}) copy-start(bf16[128,128]{1,0:T(8,128)(2,1)} %reduce-scatter.4.cloned.1.call-done) | copy-start | bytes 98308
  402.9 54.5 %copy-start.16 = (f32[128,512]{1,0:T(8,128)S(1)}, f32[128,512]{1,0:T(8,128)}, u32[]{:S(2)}) copy-start(f32[128,512]{1,0:T(8,128)} %get-tuple-element.171) | copy-start | bytes 786436
  404.0 314.1 %all-reduce.4.cloned.1.call-start = ((), (), s32[]{:S(2)}) async-start(), calls=%async_computation.8 | async-start | bytes 1048576 | tf_op jit(solution)/shard_map/psum | solution.py:137
  416.3 43.2 %copy-start.4 = (bf16[128,512]{1,0:T(8,128)(2,1)S(1)}, bf16[128,512]{1,0:T(8,128)(2,1)}, u32[]{:S(2)}) copy-start(bf16[128,512]{1,0:T(8,128)(2,1)} %reduce-scatter.6.cloned.1.call-done) | copy-start | bytes 393220
Sparse Core Ops, SparseCore 0:
  84.8 84.2 reduce-scatter.3
  209.7 37.6 all-gather.2
  250.0 49.1 all-gather.4
  327.7 88.5 reduce-scatter.5
  418.6 38.7 reduce-scatter.7
  463.4 254.5 all-reduce.3
where the time goes:
time: 730 us; the launch traced here: 728 us
  waiting for transfers between devices  346 us (47%)
  blocking collectives  148 us (20%)
  other arithmetic  116 us (16%)
  matrix products  55 us (8%)
  local copies, waits for them, and re-layouts  47.4 us (6%)
  between operations  15.6 us (2%)
    psum x1, waiting for transfers between devices, local(): lax.psum((first_term * node_scale, second_term * node_scale), ('row', 'co...  258 us
    unnamed x1, blocking collectives  119 us
    scatter-add x10, other arithmetic, forward_accumulate(): return (running.at[rows_here].add(contrib), None)  64.6 us
    reduce_scatter x1, waiting for transfers between devices, local(): lax.psum_scatter(backward_part(tile_values, col_index, row_index, grad_ro...  39.2 us
    all_gather x1, waiting for transfers between devices, local(): panel_hidden = lax.all_gather(hidden, 'row', axis=0, tiled=True)  36.8 us
    scatter-add x5, other arithmetic, backward_accumulate(): return (running.at[cols_here].add(contrib), None)  30.8 us
    all_gather x1, blocking collectives, local(): panel_in = lax.all_gather(features, 'row', axis=0, tiled=True)  28.8 us
    dot_general x10, matrix products, forward_accumulate(): jnp.einsum('sij,sjf->sif', values_here, source_blocks[cols_here], preferr...  25 us
  transfers between devices with their start and end apart: 6, of which 4 were waited for; matrix products, arithmetic and copies ran while one was open for 22% of the time, Pallas kernels for 0%

commit v1 on v0

--- a/solution.py
+++ b/solution.py
@@ -99,7 +99,9 @@
     degree_part = (
         jnp.zeros((row_groups, BLOCK), jnp.float32).at[row_index].add(row_sums).reshape(-1)
     )
-    panel_in = lax.all_gather(features, "row", axis=0, tiled=True)
+    panel_in = jnp.concatenate(
+        lax.all_to_all(jnp.stack([features] * lax.axis_size("row")), "row", 0, 0), axis=0
+    )
     partial_in = forward_part(tile_values, row_index, col_index, panel_in, row_groups)
     degree = lax.psum_scatter(degree_part, "col", scatter_dimension=0, tiled=True)
     summed_in = lax.psum_scatter(

time: 730 us -> 718 us (0.984)
  blocking collectives: 148 us -> 123 us
  starting transfers between devices: 0.24 us -> 8.71 us
    all_gather x1 -> x0, blocking collectives: 28.8 us -> none  [local(): panel_in = lax.all_gather(features, 'row', axis=0, tiled=True)]
    all_to_all x0 -> x1, starting transfers between devices: none -> 8.47 us  [local(): lax.all_to_all(jnp.stack([features] * lax.axis_size('row')), 'row', 0, 0)]
  transfers between devices with their start and end apart: 6 -> 7, of which waited for: 4 -> 4; matrix products, arithmetic and copies ran while one was open for 22% -> 25% of each run, Pallas kernels for 0% -> 0%
where the time goes in v1:
time: 718 us; the launch traced here: 716 us
  waiting for transfers between devices  348 us (48%)
  blocking collectives  123 us (17%)
  other arithmetic  116 us (16%)
  matrix products  55 us (8%)
  local copies, waits for them, and re-layouts  49 us (7%)
  between operations  15.6 us (2%)
  starting transfers between devices  8.71 us (1%)
    psum x1, waiting for transfers between devices, local(): lax.psum((first_term * node_scale, second_term * node_scale), ('row', 'co...  258 us
    unnamed x1, blocking collectives  123 us
    scatter-add x10, other arithmetic, forward_accumulate(): return (running.at[rows_here].add(contrib), None)  64.7 us
    reduce_scatter x1, waiting for transfers between devices, local(): lax.psum_scatter(backward_part(tile_values, col_index, row_index, grad_ro...  39.1 us
    all_gather x1, waiting for transfers between devices, local(): panel_hidden = lax.all_gather(hidden, 'row', axis=0, tiled=True)  38.9 us
    scatter-add x5, other arithmetic, backward_accumulate(): return (running.at[cols_here].add(contrib), None)  30.8 us
    dot_general x10, matrix products, forward_accumulate(): jnp.einsum('sij,sjf->sif', values_here, source_blocks[cols_here], preferr...  25 us
    dot_general x5, matrix products, backward_accumulate(): jnp.einsum('sij,sif->sjf', values_here, source_blocks[rows_here], preferr...  22.6 us
  transfers between devices with their start and end apart: 7, of which 4 were waited for; matrix products, arithmetic and copies ran while one was open for 25% of the time, Pallas kernels for 0%

profile of v1, /device:TPU:2, one launch (start us, length us, event | category | flops | bytes accessed | tf_op | source)
XLA Modules:
  0.0 715.6 jit_solution(15841755999399568132)
XLA Ops:
  8.7 8.5 %all-to-all-start = ((bf16[8,128,128]{2,1,0:T(8,128)(2,1)}), bf16[8,128,128]{2,1,0:T(8,128)(2,1)S(1)}, u32[]{:S(2)}, u32[]{:S(2)}) async-start(bf16[8,128,128]{2,1,0:T(8,128)(2,1)} %stack.2), calls=%async_computation | async-start | bytes 524288 | tf_op jit(solution)/shard_map/all_to_all | solution.py:103
  36.3 26.8 %while.30 = (s32[]{:T(128)}, f32[32,128,128]{2,1,0:T(8,128)}, s32[5,16]{1,0:T(8,128)S(1)}, bf16[5,16,128,128]{3,2,1,0:T(8,128)(2,1)}, s32[5,16]{1,0:T(8,128)S(1)}, /*index=5*/bf16[8,128,128]{2,1,0:T(8,128)(2,1)S(1)}, s32[]{:T(128)}) while((s32[]{:T(128)}, f32[32,128,128]{2,1,0:T(8,128)}, s32[5,16]{1,0:T(8,128)S(1)}, ...), condition=%wide.region_5.6_spmd, body=%wide.region_3.0_spmd.sunk | while | flops 67372128 | bytes 6296093 | solution.py:48
  70.1 123.0 %all-reduce = f32[4096]{0:T(1024)S(1)} all-reduce(f32[4096]{0:T(1024)S(1)} %bitcast.120), channel_id=2, replica_groups=mesh['row'=8,'col'=32] {'col'}, use_global_device_ids=true, to_apply=%region_2.3.clone | all-reduce | flops 4096 | bytes 32768
  195.9 38.9 %all-gather.3.cloned.1.call-done = bf16[1024,512]{1,0:T(8,128)(2,1)} async-done(((bf16[128,512]{1,0:T(8,128)(2,1)}), bf16[1024,512]{1,0:T(8,128)(2,1)}) %all-gather.3.cloned.1.call-update) | async-done | bytes 1048592 | tf_op jit(solution)/shard_map/all_gather | solution.py:114
  239.2 69.8 %while.31 = (s32[]{:T(128)}, f32[32,128,512]{2,1,0:T(8,128)}, s32[5,16]{1,0:T(8,128)S(1)}, bf16[5,16,128,128]{3,2,1,0:T(8,128)(2,1)}, s32[5,16]{1,0:T(8,128)S(1)}, /*index=5*/bf16[8,128,512]{2,1,0:T(8,128)(2,1)S(1)}, s32[]{:T(128)}) while((s32[]{:T(128)}, f32[32,128,512]{2,1,0:T(8,128)}, s32[5,16]{1,0:T(8,128)S(1)}, ...), condition=%wide.region_9.10_spmd, body=%wide.region_7.9_spmd.sunk | while | flops 269485152 | bytes 23597596 | solution.py:48
  243.5 9.5 %scatter_fusion.1 = f32[32,128,512]{2,1,0:T(8,128)} fusion(f32[32,128,512]{2,1,0:T(8,128)} %get-tuple-element.326, s32[16]{0:T(128)S(1)} %get-tuple-element.287, f32[16,128,512]{2,1,0:T(8,128)} %fusion.71), kind=kCustom, calls=%fused_computation.4.clone.1 | custom fusion | flops 1048576 | bytes 12582976 | tf_op jit(solution)/shard_map/while/body/eval_jaxpr/scatter-add | solution.py:45
  257.4 9.6 %scatter_fusion.1 = f32[32,128,512]{2,1,0:T(8,128)} fusion(f32[32,128,512]{2,1,0:T(8,128)} %get-tuple-element.326, s32[16]{0:T(128)S(1)} %get-tuple-element.287, f32[16,128,512]{2,1,0:T(8,128)} %fusion.71), kind=kCustom, calls=%fused_computation.4.clone.1 | custom fusion | flops 1048576 | bytes 12582976 | tf_op jit(solution)/shard_map/while/body/eval_jaxpr/scatter-add | solution.py:45
  271.4 9.7 %scatter_fusion.1 = f32[32,128,512]{2,1,0:T(8,128)} fusion(f32[32,128,512]{2,1,0:T(8,128)} %get-tuple-element.326, s32[16]{0:T(128)S(1)} %get-tuple-element.287, f32[16,128,512]{2,1,0:T(8,128)} %fusion.71), kind=kCustom, calls=%fused_computation.4.clone.1 | custom fusion | flops 1048576 | bytes 12582976 | tf_op jit(solution)/shard_map/while/body/eval_jaxpr/scatter-add | solution.py:45
  285.4 9.7 %scatter_fusion.1 = f32[32,128,512]{2,1,0:T(8,128)} fusion(f32[32,128,512]{2,1,0:T(8,128)} %get-tuple-element.326, s32[16]{0:T(128)S(1)} %get-tuple-element.287, f32[16,128,512]{2,1,0:T(8,128)} %fusion.71), kind=kCustom, calls=%fused_computation.4.clone.1 | custom fusion | flops 1048576 | bytes 12582976 | tf_op jit(solution)/shard_map/while/body/eval_jaxpr/scatter-add | solution.py:45
  299.5 9.5 %scatter_fusion.1 = f32[32,128,512]{2,1,0:T(8,128)} fusion(f32[32,128,512]{2,1,0:T(8,128)} %get-tuple-element.326, s32[16]{0:T(128)S(1)} %get-tuple-element.287, f32[16,128,512]{2,1,0:T(8,128)} %fusion.71), kind=kCustom, calls=%fused_computation.4.clone.1 | custom fusion | flops 1048576 | bytes 12582976 | tf_op jit(solution)/shard_map/while/body/eval_jaxpr/scatter-add | solution.py:45
  309.0 5.9 convert_element_type.91
  315.3 75.0 %while.32 = (s32[]{:T(128)}, f32[8,128,512]{2,1,0:T(8,128)S(1)}, s32[5,16]{1,0:T(8,128)S(1)}, bf16[5,16,128,128]{2,3,1,0:T(8,128)(2,1)}, s32[5,16]{1,0:T(8,128)S(1)}, /*index=5*/bf16[32,128,512]{2,1,0:T(8,128)(2,1)}, s32[]{:T(128)}) while((s32[]{:T(128)}, f32[8,128,512]{2,1,0:T(8,128)S(1)}, s32[5,16]{1,0:T(8,128)S(1)}, ...), condition=%wide.region_13.14_spmd, body=%wide.region_11.13_spmd.sunk | while | flops 269485152 | bytes 23597596 | solution.py:69
  323.9 6.2 scatter_fusion.2
  334.5 4.5 fusion.75
  339.0 6.2 scatter_fusion.2
  349.6 4.5 fusion.75
  354.1 6.1 scatter_fusion.2
  364.4 4.8 fusion.75
  369.2 6.2 scatter_fusion.2
  379.7 4.5 fusion.75
  384.1 6.1 scatter_fusion.2
  391.5 12.2 %reduce-scatter.6.cloned.1.call-done = bf16[128,512]{1,0:T(8,128)(2,1)} async-done(((bf16[4096,512]{1,0:T(8,128)(2,1)}), bf16[128,512]{1,0:T(8,128)(2,1)}) %reduce-scatter.6.cloned.1.call-update) | async-done | bytes 131088 | tf_op jit(solution)/shard_map/reduce_scatter | solution.py:116
  405.6 39.1 %reduce-scatter.8.cloned.1.call-done = bf16[128,512]{1,0:T(8,128)(2,1)} async-done(((bf16[1024,512]{1,0:T(8,128)(2,1)}), bf16[128,512]{1,0:T(8,128)(2,1)}) %reduce-scatter.8.cloned.1.call-update) | async-done | bytes 131088 | tf_op jit(solution)/shard_map/reduce_scatter | solution.py:126
  447.6 257.8 %all-reduce.4.cloned.1.call-done = (f32[128,512]{1,0:T(8,128)}, f32[512,128]{1,0:T(8,128)}) async-done(((f32[128,512]{1,0:T(8,128)}, f32[512,128]{1,0:T(8,128)}), (f32[128,512]{1,0:T(8,128)}, f32[512,128]{1,0:T(8,128)})) %all-reduce.4.cloned.1.call-update) | async-done | bytes 524304 | tf_op jit(solution)/shard_map/psum | solution.py:139
  (140 shorter events, 117.3 us)
Async XLA Ops:
  7.2 187.8 %copy-start = (bf16[512,128]{1,0:T(8,128)(2,1)S(1)}, bf16[512,128]{1,0:T(8,128)(2,1)}, u32[]{:S(2)}) copy-start(bf16[512,128]{1,0:T(8,128)(2,1)} %param.17) | copy-start | bytes 393220
  8.7 26.0 %all-to-all-start = ((bf16[8,128,128]{2,1,0:T(8,128)(2,1)}), bf16[8,128,128]{2,1,0:T(8,128)(2,1)S(1)}, u32[]{:S(2)}, u32[]{:S(2)}) async-start(bf16[8,128,128]{2,1,0:T(8,128)(2,1)} %stack.2), calls=%async_computation | async-start | bytes 524288 | tf_op jit(solution)/shard_map/all_to_all | solution.py:103
  17.2 176.0 %reduce-scatter.4.cloned.1.call-start = ((), (), s32[]{:S(2)}) async-start(), calls=%async_computation.4 | async-start | bytes 1081344 | tf_op jit(solution)/shard_map/reduce_scatter | solution.py:107
  63.1 3.0 copy-start.15
  63.1 4.3 copy-start.14
  63.1 4.3 copy-start.5
  63.1 4.3 copy-start.2
  66.0 127.2 %copy-start.8 = (bf16[128,128]{1,0:T(8,128)(2,1)S(1)}, bf16[128,128]{1,0:T(8,128)(2,1)}, u32[]{:S(2)}) copy-start(bf16[128,128]{1,0:T(8,128)(2,1)} %param.15) | copy-start | bytes 98308
  66.0 127.2 %copy-start.12 = (bf16[128,512]{1,0:T(8,128)(2,1)S(1)}, bf16[128,512]{1,0:T(8,128)(2,1)}, u32[]{:S(2)}) copy-start(bf16[128,512]{1,0:T(8,128)(2,1)} %param.16) | copy-start | bytes 393220
  66.0 129.0 %copy-start.6 = (bf16[128,128]{1,0:T(8,128)(2,1)S(1)}, bf16[128,128]{1,0:T(8,128)(2,1)}, u32[]{:S(2)}) copy-start(bf16[128,128]{1,0:T(8,128)(2,1)} %param.23) | copy-start | bytes 98308
  66.0 168.8 %all-gather.3.cloned.1.call-start = ((), (), s32[]{:S(2)}) async-start(), calls=%async_computation.5 | async-start | bytes 1179648 | tf_op jit(solution)/shard_map/all_gather | solution.py:114
  193.2 46.0 %copy-start.10 = (f32[128]{0:T(128)}, f32[128]{0:T(128)S(1)}, u32[]{:S(2)}) copy-start(f32[128]{0:T(128)S(1)} %fusion.37) | copy-start | bytes 1540
  195.0 120.1 %all-gather.5.cloned.1.call-start = ((), (), s32[]{:S(2)}) async-start(), calls=%async_computation.7 | async-start | bytes 4325376 | tf_op jit(solution)/shard_map/all_gather | solution.py:125
  195.9 207.8 %reduce-scatter.6.cloned.1.call-start = ((), (), s32[]{:S(2)}) async-start(), calls=%async_computation.6 | async-start | bytes 4325376 | tf_op jit(solution)/shard_map/reduce_scatter | solution.py:116
  234.9 4.3 copy-start.1
  314.9 129.8 %reduce-scatter.8.cloned.1.call-start = ((), (), s32[]{:S(2)}) async-start(), calls=%async_computation.8 | async-start | bytes 1179648 | tf_op jit(solution)/shard_map/reduce_scatter | solution.py:126
  390.3 13.4 %copy-start.3 = (bf16[128,512]{1,0:T(8,128)(2,1)S(1)}, bf16[128,512]{1,0:T(8,128)(2,1)}, u32[]{:S(2)}) copy-start(bf16[128,512]{1,0:T(8,128)(2,1)} %get-tuple-element.170) | copy-start | bytes 393220
  390.3 13.4 %copy-start.7 = (bf16[128,128]{1,0:T(8,128)(2,1)S(1)}, bf16[128,128]{1,0:T(8,128)(2,1)}, u32[]{:S(2)}) copy-start(bf16[128,128]{1,0:T(8,128)(2,1)} %param.23) | copy-start | bytes 98308
  390.3 13.4 %copy-start.11 = (f32[128]{0:T(128)S(1)}, f32[128]{0:T(128)}, u32[]{:S(2)}) copy-start(f32[128]{0:T(128)} %copy-done.10) | copy-start | bytes 1540
  390.3 54.4 %copy-start.9 = (bf16[128,128]{1,0:T(8,128)(2,1)S(1)}, bf16[128,128]{1,0:T(8,128)(2,1)}, u32[]{:S(2)}) copy-start(bf16[128,128]{1,0:T(8,128)(2,1)} %param.15) | copy-start | bytes 98308
  390.3 54.4 %copy-start.13 = (bf16[128,128]{1,0:T(8,128)(2,1)S(1)}, bf16[128,128]{1,0:T(8,128)(2,1)}, u32[]{:S(2)}) copy-start(bf16[128,128]{1,0:T(8,128)(2,1)} %reduce-scatter.4.cloned.1.call-done) | copy-start | bytes 98308
  390.3 54.4 %copy-start.16 = (f32[128,512]{1,0:T(8,128)S(1)}, f32[128,512]{1,0:T(8,128)}, u32[]{:S(2)}) copy-start(f32[128,512]{1,0:T(8,128)} %get-tuple-element.171) | copy-start | bytes 786436
  391.5 314.0 %all-reduce.4.cloned.1.call-start = ((), (), s32[]{:S(2)}) async-start(), calls=%async_computation.9 | async-start | bytes 1048576 | tf_op jit(solution)/shard_map/psum | solution.py:139
  403.7 43.1 %copy-start.4 = (bf16[128,512]{1,0:T(8,128)(2,1)S(1)}, bf16[128,512]{1,0:T(8,128)(2,1)}, u32[]{:S(2)}) copy-start(bf16[128,512]{1,0:T(8,128)(2,1)} %reduce-scatter.6.cloned.1.call-done) | copy-start | bytes 393220
Sparse Core Ops, SparseCore 0:
  66.2 86.6 reduce-scatter.3
  195.1 39.7 all-gather.2
  237.4 49.1 all-gather.4
  315.1 88.5 reduce-scatter.5
  406.0 38.6 reduce-scatter.7
  450.8 254.6 all-reduce.3
